TPU v7x, 32 devices: a whole 2x2x4 slice. The times are simulated.
32 devices in a mesh: section: 2 (over x), mp: 4 (over z), dp: 4 (over y, core).
Axes of the slice: x: 2, y: 2, z: 4, core: 2. Of those that a mesh axis runs over, the one named last changes fastest.
Arguments:
- text_in: bfloat16 [4, 2, 512, 8192], P('dp', 'section', None, 'mp'), may hold values from -6 to 6
- vision: bfloat16 [4, 2, 256, 8192], P('dp', 'section', None, 'mp'), may hold values from -6 to 6
- tile_counts: int32 [4, 2], P('dp'), may hold values from 1 to 4, as said below
- lengths: int32 [4, 2], P('dp', 'section'), may hold values from 128 to 512, as said below
- image_of: int32 [4, 2], P('dp'), may hold values from 0 to 1, each once within a row
- norm_gain: float32 [2, 8192], P('section'), may hold values from 0.5 to 1.5
- query_weight: bfloat16 [2, 8192, 4096], P('section', 'dp', 'mp'), may hold values from -0.0625 to 0.0625
- key_weight: bfloat16 [2, 8192, 1024], P('section', 'dp', 'mp'), may hold values from -0.0625 to 0.0625
- value_weight: bfloat16 [2, 8192, 1024], P('section', 'dp', 'mp'), may hold values from -0.0625 to 0.0625
- query_gain: float32 [2, 128], P('section')
- key_gain: float32 [2, 128], P('section')
- cross_gate: float32 [2], P('section'), may hold values from 0.4 to 1.5
- context_grad: bfloat16 [4, 2, 512, 4096], P('dp', 'section', None, 'mp'), may hold values from -6 to 6
Outputs:
- gated_context: bfloat16 [4, 2, 512, 4096], P('dp', 'section', None, 'mp')
- vision_grad: bfloat16 [4, 2, 256, 8192], P('dp', 'section', None, 'mp')
- key_weight_grad: bfloat16 [2, 8192, 1024], P('section', 'dp', 'mp')
- value_weight_grad: bfloat16 [2, 8192, 1024], P('section', 'dp', 'mp')
Inputs may be any that keep to these rules, and one draw needn't show every extreme that they name: `tile_counts`: some image has 4 tiles and some has one. `lengths`: some sample has the full 512 tokens. `image_of`: each row is a permutation of the sections.
All inputs are finite; a program needn't handle non-finite values.
Results may differ from a plain program's by a relative error of at most 0.018.
Values may be sent and summed in bfloat16 or wider, within the bound.
No kernel may reach another device: no remote copies, remote signals or barrier semaphores. Data moves between devices by JAX's collectives and lax.ppermute only.
A program may use at most 192 MiB of HBM per device.

v0:
```python
import jax
import jax.numpy as jnp
from jax import lax
from jax.sharding import PartitionSpec as P

HD = 128
TILE_ROWS = 64


def shifted(value, axis, steps):
    count = lax.axis_size(axis)
    pairs = [(source, (source + steps) % count) for source in range(count)]
    return lax.ppermute(value, axis, pairs)


def norm_rows(values, gain):
    values = values.astype(jnp.float32)
    scaled = values * lax.rsqrt(jnp.mean(values * values, axis=-1, keepdims=True) + 1e-05)
    return scaled * gain


def rounded(values):
    return lax.optimization_barrier(values.astype(jnp.bfloat16)).astype(jnp.float32)


def attend(queries, keys_raw, values_raw, key_norm, usable, present, gate_value):
    keys = rounded(norm_rows(keys_raw, key_norm))
    values = rounded(values_raw)
    text_rows, heads, depth = queries.shape
    groups = keys.shape[1]
    grouped = queries.astype(jnp.float32).reshape(text_rows, groups, heads // groups, depth)
    scores = jnp.einsum("tgjd,vgd->gjtv", grouped, keys) * depth ** (-0.5)
    scores = jnp.where(usable[None, None, None, :], scores, -1e30)
    highest = lax.stop_gradient(jnp.max(scores, axis=-1, keepdims=True))
    weights = jnp.exp(scores - highest)
    probs = rounded(weights / jnp.sum(weights, axis=-1, keepdims=True))
    context = jnp.einsum("gjtv,vgd->tgjd", probs, values).reshape(text_rows, heads * depth)
    return jnp.where(present[:, None], jnp.tanh(gate_value) * context, 0.0)


def per_device(
    text_in,
    vision,
    tile_counts,
    lengths,
    image_of,
    norm_gain,
    query_weight,
    key_weight,
    value_weight,
    query_gain,
    key_gain,
    cross_gate,
    context_grad,
):
    arrived = shifted(text_in, "section", 1)
    full_text = lax.all_gather(arrived, "mp", axis=3, tiled=True)[0, 0]
    text_rows = full_text.shape[0]
    normed = norm_rows(full_text, norm_gain[0]).astype(jnp.bfloat16)
    width_q = query_weight.shape[2]
    columns = normed
    query_raw = jnp.dot(
        columns,
        lax.all_gather(query_weight, "dp", axis=1, tiled=True)[0],
        preferred_element_type=jnp.float32,
    )
    queries = norm_rows(query_raw.reshape(text_rows, width_q // HD, HD), query_gain[0]).astype(
        jnp.bfloat16
    )
    key_full, value_full = (
        lax.all_gather(key_weight, "dp", axis=1, tiled=True),
        lax.all_gather(value_weight, "dp", axis=1, tiled=True),
    )
    key_full = key_full[0]
    value_full = value_full[0]
    slot_rows = vision.shape[2]
    part_width = vision.shape[3]
    wanted = image_of[0, lax.axis_index("section")]
    shard_piece = lax.all_gather(vision, "section", axis=1, tiled=True)
    owners = jnp.arange(shard_piece.shape[1])
    chosen = (owners == wanted)[:, None, None]
    taken = jnp.where(chosen, shard_piece[0], jnp.zeros_like(shard_piece[0]))
    image_part = jnp.sum(taken.astype(jnp.float32), axis=0).astype(jnp.bfloat16)
    image = lax.all_gather(image_part, "mp", axis=1, tiled=True)
    width_k = key_full.shape[1]
    keys_raw = jnp.dot(image, key_full, preferred_element_type=jnp.float32).reshape(
        slot_rows, width_k // HD, HD
    )
    values_raw = jnp.dot(image, value_full, preferred_element_type=jnp.float32).reshape(
        slot_rows, width_k // HD, HD
    )
    usable = jnp.arange(slot_rows) < tile_counts[0, wanted] * TILE_ROWS
    present = jnp.arange(text_rows) < lengths[0, 0]

    def forward(keys_in, values_in):
        return attend(queries, keys_in, values_in, key_gain[0], usable, present, cross_gate[0])

    context, pullback = jax.vjp(forward, keys_raw, values_raw)
    gated_context = context.astype(jnp.bfloat16).reshape(1, 1, text_rows, width_q)
    key_back, value_back = pullback(context_grad[0, 0].astype(jnp.float32))
    key_flat = key_back.reshape(slot_rows, width_k).astype(jnp.bfloat16)
    value_flat = value_back.reshape(slot_rows, width_k).astype(jnp.bfloat16)
    contract = (((1,), (1,)), ((), ()))
    partial_sum = lax.dot_general(key_flat, key_full, contract, preferred_element_type=jnp.float32)
    partial_sum = partial_sum + lax.dot_general(
        value_flat, value_full, contract, preferred_element_type=jnp.float32
    )
    partial_bf = partial_sum.astype(jnp.bfloat16)
    summed = lax.psum_scatter(
        partial_bf.astype(jnp.float32).astype(jnp.bfloat16), "mp", scatter_dimension=1, tiled=True
    )
    row_ids = jnp.arange(slot_rows * lax.axis_size("section"))
    taken = jnp.take(summed, row_ids % slot_rows, axis=0).astype(jnp.float32)
    routed = lax.psum_scatter(
        jnp.where((row_ids // slot_rows == wanted)[:, None], taken, 0.0).astype(jnp.bfloat16),
        "section",
        scatter_dimension=0,
        tiled=True,
    )
    vision_grad = routed.reshape(1, 1, slot_rows, part_width)
    columns = image
    inner = (((0,), (0,)), ((), ()))
    key_part = lax.dot_general(columns, key_flat, inner, preferred_element_type=jnp.float32).astype(
        jnp.bfloat16
    )
    value_part = lax.dot_general(
        columns, value_flat, inner, preferred_element_type=jnp.float32
    ).astype(jnp.bfloat16)
    both_grads = lax.psum_scatter(
        jnp.concatenate([key_part, value_part], axis=1).astype(jnp.float32).astype(jnp.bfloat16),
        "dp",
        scatter_dimension=0,
        tiled=True,
    )
    key_weight_grad = both_grads[:, :width_k][None]
    value_weight_grad = both_grads[:, width_k:][None]
    return (gated_context, vision_grad, key_weight_grad, value_weight_grad)


def solution(mesh):
    return jax.shard_map(
        per_device,
        mesh=mesh,
        in_specs=(
            P("dp", "section", None, "mp"),
            P("dp", "section", None, "mp"),
            P("dp", None),
            P("dp", "section"),
            P("dp", None),
            P("section", None),
            P("section", "dp", "mp"),
            P("section", "dp", "mp"),
            P("section", "dp", "mp"),
            P("section", None),
            P("section", None),
            P("section"),
            P("dp", "section", None, "mp"),
        ),
        out_specs=(
            P("dp", "section", None, "mp"),
            P("dp", "section", None, "mp"),
            P("section", "dp", "mp"),
            P("section", "dp", "mp"),
        ),
        check_vma=False,
    )
```

profile of v0, /device:TPU:0, one launch (start us, length us, event | category | flops | bytes accessed | tf_op | source)
XLA Modules:
  0.0 705.0 jit_solution(10474390815657424555)
XLA Ops:
  7.2 0.7 all-gather.7.cloned.1.call-update
  8.0 0.7 all-gather.13.cloned.1.call-update
  8.7 0.7 all-gather.11.cloned.1.call-update
  9.5 0.6 constant_dynamic-slice_fusion.1
  10.0 0.6 iota_compare_fusion.2
  10.7 34.7 %all-gather.7.cloned.1.call-done = bf16[1,2,256,2048]{3,2,0,1:T(8,128)(2,1)} async-done(((bf16[1,1,256,2048]{3,2,0,1:T(8,128)(2,1)}), bf16[1,2,256,2048]{3,2,0,1:T(8,128)(2,1)}) %all-gather.7.cloned.1.call-update) | async-done | bytes 2097168 | tf_op jit(solution)/shard_map/all_gather | solution.py:79
  45.4 3.4 fusion.34
  49.3 47.3 %collective-permute-done = bf16[1,1,512,2048]{3,2,1,0:T(8,128)(2,1)S(1)} collective-permute-done((bf16[1,1,512,2048]{3,2,1,0:T(8,128)(2,1)}, bf16[1,1,512,2048]{3,2,1,0:T(8,128)(2,1)S(1)}, u32[]{:S(2)}, u32[]{:S(2)}) %collective-permute-start) | collective-permute-done | bytes 2097184 | tf_op jit(solution)/shard_map/ppermute | solution.py:13
  96.5 1.4 copy-done.11
  99.9 0.5 copy.81
  102.4 0.6 fusion.100
  103.0 1.2 iota_compare_fusion.1
  104.2 6.4 copy.51
  110.6 7.0 all-gather.11.cloned.1.call-done
  117.6 6.4 copy.50
  123.9 76.4 %all-gather.9.cloned.1.call-done = bf16[256,8192]{1,0:T(8,128)(2,1)} async-done(((bf16[256,2048]{1,0:T(8,128)(2,1)}), bf16[256,8192]{1,0:T(8,128)(2,1)}) %all-gather.9.cloned.1.call-update) | async-done | bytes 4194320 | tf_op jit(solution)/shard_map/all_gather | solution.py:84
  200.4 4.9 multiply_reduce_fusion.2
  205.3 0.7 multiply_convert_fusion.1
  206.3 1.3 fusion.60
  207.6 2.0 fusion.43
  209.6 140.3 %all-gather.15.cloned.1.call-done = bf16[1,1,512,8192]{3,2,1,0:T(8,128)(2,1)} async-done(((bf16[1,1,512,2048]{3,2,1,0:T(8,128)(2,1)}), bf16[1,1,512,8192]{3,2,1,0:T(8,128)(2,1)}) %all-gather.15.cloned.1.call-update) | async-done | bytes 8388624 | tf_op jit(solution)/shard_map/all_gather | solution.py:57
  350.0 5.1 fusion.1
  355.1 100.4 %all-gather.17.cloned.1.call-done = bf16[1,8192,1024]{2,1,0:T(8,128)(2,1)} async-done(((bf16[1,2048,1024]{2,1,0:T(8,128)(2,1)}), bf16[1,8192,1024]{2,1,0:T(8,128)(2,1)}) %all-gather.17.cloned.1.call-update) | async-done | bytes 16777232 | tf_op jit(solution)/shard_map/all_gather | solution.py:64
  455.5 21.4 %copy.52 = bf16[1024,8192]{1,0:T(8,128)(2,1)} copy(bf16[1024,8192]{0,1:T(8,128)(2,1)} %bitcast.150) | data formatting | bytes 33554432 | tf_op jit(solution)/shard_map/dot_general | solution.py:62
  477.0 14.8 %multiply_reduce_fusion = (f32[512,8]{0,1:T(8,128)S(1)}, f32[512,8,128]{0,2,1:T(8,128)S(1)}) fusion(bf16[8,128,8192]{2,1,0:T(8,128)(2,1)} %bitcast.151, bf16[1,1,512,8192]{3,2,1,0:T(8,128)(2,1)} %all-gather.15.cloned.1.call-done, f32[8192]{0:T(1024)S(1)} %bitcast.169, f32[512]{0:T(512)S(1)} %add_rsqrt_fusion.1), kind=kOutput, calls=%fused_computation.55 | convolution fusion | flops 8607756288 | bytes 27314176 | tf_op jit(solution)/shard_map/dot_general | solution.py:62
  492.3 5.1 fusion.101
  497.4 0.7 multiply_divide_fusion
  498.1 3.9 fusion.16
  502.0 0.7 copy-done.9
  502.8 1.2 fusion.66
  504.3 0.8 fusion.63
  505.1 1.1 copy-done.4
  506.2 1.3 fusion.19
  507.5 0.9 copy-done.7
  508.4 3.4 fusion.4
  511.9 5.5 convolution_convert_fusion
  517.4 3.2 convolution_convert_fusion.1
  520.6 7.7 %pad_maximum_fusion = bf16[8192,512]{0,1:T(8,128)(2,1)} fusion(bf16[8192,256]{0,1:T(8,128)(2,1)} %convolution_convert_fusion, bf16[8192,256]{0,1:T(8,128)(2,1)} %convolution_convert_fusion.1), kind=kLoop, calls=%fused_computation.13 | loop fusion | flops 16777216 | bytes 16777216 | tf_op jit(solution)/shard_map/concatenate | solution.py:130
  528.4 0.7 fusion.89
  529.1 59.6 %reduce-scatter.4.cloned.1.call-done = bf16[256,2048]{1,0:T(8,128)(2,1)} async-done(((bf16[256,8192]{1,0:T(8,128)(2,1)}), bf16[256,2048]{1,0:T(8,128)(2,1)}) %reduce-scatter.4.cloned.1.call-update) | async-done | bytes 1048592 | tf_op jit(solution)/shard_map/reduce_scatter | solution.py:109
  588.7 6.8 gather_fusion
  595.5 3.7 select_convert_fusion
  600.3 1.2 select_convert_fusion.1
  601.6 62.2 %reduce-scatter.8.cloned.1.call-done = bf16[2048,512]{0,1:T(8,128)(2,1)} async-done(((bf16[8192,512]{0,1:T(8,128)(2,1)}), bf16[2048,512]{0,1:T(8,128)(2,1)}) %reduce-scatter.8.cloned.1.call-update) | async-done | bytes 2097168 | tf_op jit(solution)/shard_map/reduce_scatter | solution.py:129
  663.8 1.7 slice_bitcast_fusion
  665.4 1.3 copy.64
  666.7 1.3 copy.65
  668.0 30.4 %reduce-scatter.6.cloned.1.call-done = bf16[256,2048]{1,0:T(8,128)(2,1)} async-done(((bf16[512,2048]{1,0:T(8,128)(2,1)}), bf16[256,2048]{1,0:T(8,128)(2,1)}) %reduce-scatter.6.cloned.1.call-update) | async-done | bytes 1048592 | tf_op jit(solution)/shard_map/reduce_scatter | solution.py:114
  (65 shorter events, 3.5 us)
Async XLA Ops:
  7.2 2.3 copy-start
  7.2 38.2 %all-gather.7.cloned.1.call-start = ((), (), s32[]{:S(2)}) async-start(), calls=%async_computation.3 | async-start | bytes 3145728 | tf_op jit(solution)/shard_map/all_gather | solution.py:79
  7.9 96.3 %all-gather.13.cloned.1.call-start = ((), (), s32[]{:S(2)}) async-start(), calls=%async_computation.6 | async-start | bytes 5242880 | tf_op jit(solution)/shard_map/all_gather | solution.py:71
  8.7 108.9 %all-gather.11.cloned.1.call-start = ((), (), s32[]{:S(2)}) async-start(), calls=%async_computation.5 | async-start | bytes 5242880 | tf_op jit(solution)/shard_map/all_gather | solution.py:72
  9.4 191.0 %all-gather.9.cloned.1.call-start = ((), (), s32[]{:S(2)}) async-start(), calls=%async_computation.4 | async-start | bytes 5242880 | tf_op jit(solution)/shard_map/all_gather | solution.py:84
  48.8 51.1 %copy-start.12 = (bf16[1,1,512,1024]{3,2,1,0:T(8,128)(2,1)S(1)}, bf16[1,1,512,1024]{3,2,1,0:T(8,128)(2,1)}, u32[]{:S(2)}) copy-start(bf16[1,1,512,1024]{3,2,1,0:T(8,128)(2,1)} %param.25) | copy-start | bytes 3145732
  48.8 301.2 %all-gather.15.cloned.1.call-start = ((), (), s32[]{:S(2)}) async-start(), calls=%async_computation.7 | async-start | bytes 10485760 | tf_op jit(solution)/shard_map/all_gather | solution.py:57
  48.9 47.6 %collective-permute-start = (bf16[1,1,512,2048]{3,2,1,0:T(8,128)(2,1)}, bf16[1,1,512,2048]{3,2,1,0:T(8,128)(2,1)S(1)}, u32[]{:S(2)}, u32[]{:S(2)}) collective-permute-start(bf16[1,1,512,2048]{3,2,1,0:T(8,128)(2,1)} %param.13), channel_id=1, source_target_pairs={{0,16},{16,0},{1,17},{17,1},{2,18},{18,2},{3,19},{19,3},{4,20},{20... | collective-permute-start | bytes 6291464 | tf_op jit(solution)/shard_map/ppermute | solution.py:13
  96.5 1.4 copy-start.11
  97.9 4.5 copy-start.17
  98.0 357.6 %all-gather.17.cloned.1.call-start = ((), (), s32[]{:S(2)}) async-start(), calls=%async_computation.8 | async-start | bytes 20971520 | tf_op jit(solution)/shard_map/all_gather | solution.py:64
  98.5 490.2 %reduce-scatter.4.cloned.1.call-start = ((), (), s32[]{:S(2)}) async-start(), calls=%async_computation.9 | async-start | bytes 5242880 | tf_op jit(solution)/shard_map/reduce_scatter | solution.py:109
  200.4 4.9 copy-start.14
  200.4 5.7 copy-start.5
  200.4 5.9 copy-start.10
  455.5 21.4 %copy-start.16 = (f32[1,8192]{1,0:T(1,128)S(1)}, f32[1,8192]{1,0:T(1,128)}, u32[]{:S(2)}) copy-start(f32[1,8192]{1,0:T(1,128)} %param.18) | copy-start | bytes 98308
  477.0 14.8 %copy-start.15 = (f32[1,128]{1,0:T(1,128)S(1)}, f32[1,128]{1,0:T(1,128)}, u32[]{:S(2)}) copy-start(f32[1,128]{1,0:T(1,128)} %param.22) | copy-start | bytes 1540
  498.1 3.9 copy-start.8
  498.1 4.7 copy-start.9
  498.1 4.7 copy-start.13
  498.1 4.7 copy-start.18
  502.0 2.3 copy-start.2
  504.0 2.2 copy-start.4
  506.2 2.2 copy-start.7
  511.8 151.9 %reduce-scatter.8.cloned.1.call-start = ((), (), s32[]{:S(2)}) async-start(), calls=%async_computation.11 | async-start | bytes 10485760 | tf_op jit(solution)/shard_map/reduce_scatter | solution.py:129
  511.9 5.5 copy-start.6
  528.3 170.1 %reduce-scatter.6.cloned.1.call-start = ((), (), s32[]{:S(2)}) async-start(), calls=%async_computation.10 | async-start | bytes 3145728 | tf_op jit(solution)/shard_map/reduce_scatter | solution.py:114
  595.5 3.7 copy-start.3
  600.3 98.1 %copy-start.1 = (s32[1,2]{1,0:T(1,128)S(1)}, s32[1,2]{1,0:T(1,128)}, u32[]{:S(2)}) copy-start(s32[1,2]{1,0:T(1,128)} %param.17) | copy-start | bytes 28
Sparse Core Ops, SparseCore 0:
  9.6 35.7 all-gather.6
  47.0 34.4 all-gather.12
  83.1 34.4 all-gather.10
  119.6 80.7 all-gather.8
  201.8 148.1 all-gather.14
  351.4 104.1 all-gather.16
  511.9 76.7 reduce-scatter.3
  591.5 72.2 reduce-scatter.7
  666.6 31.8 reduce-scatter.5
where the time goes:
time: 706 us; the launch traced here: 705 us
  waiting for transfers between devices  561 us (79%)
  local copies, waits for them, and re-layouts  51.3 us (7%)
  matrix products  44.1 us (6%)
  other arithmetic  30.3 us (4%)
  between operations  17.4 us (2%)
    all_gather x1, waiting for transfers between devices, per_device(): full_text = lax.all_gather(arrived, 'mp', axis=3, tiled=True)[0, 0]  140 us
    all_gather x1, waiting for transfers between devices, per_device(): lax.all_gather(query_weight, 'dp', axis=1, tiled=True)[0]  100 us
    all_gather x1, waiting for transfers between devices, per_device(): image = lax.all_gather(image_part, 'mp', axis=1, tiled=True)  76.4 us
    reduce_scatter x1, waiting for transfers between devices, per_device(): lax.psum_scatter(jnp.concatenate([key_part, value_part], axis=1).astype(j...  62.2 us
    reduce_scatter x1, waiting for transfers between devices, per_device(): lax.psum_scatter(partial_bf.astype(jnp.float32).astype(jnp.bfloat16), 'mp...  59.6 us
    ppermute x1, waiting for transfers between devices, shifted(): return lax.ppermute(value, axis, pairs)  47.3 us
    all_gather x1, waiting for transfers between devices, per_device(): shard_piece = lax.all_gather(vision, 'section', axis=1, tiled=True)  34.7 us
    reduce_scatter x1, waiting for transfers between devices, per_device(): lax.psum_scatter(jnp.where((row_ids // slot_rows == wanted)[:, None], tak...  30.4 us
  transfers between devices with their start and end apart: 10, of which 9 were waited for; matrix products, arithmetic and copies ran while one was open for 10% of the time, Pallas kernels for 0%

commit v1 on v0

--- a/solution.py
+++ b/solution.py
@@ -5,6 +5,12 @@
 
 HD = 128
 TILE_ROWS = 64
+
+
+def state_manage(xin, dim_no):
+    upper = list(xin.shape[1:])
+    upper[dim_no] *= xin.shape[0]
+    return jnp.moveaxis(xin, 0, dim_no).reshape(upper)
 
 
 def shifted(value, axis, steps):
@@ -81,7 +87,14 @@
     chosen = (owners == wanted)[:, None, None]
     taken = jnp.where(chosen, shard_piece[0], jnp.zeros_like(shard_piece[0]))
     image_part = jnp.sum(taken.astype(jnp.float32), axis=0).astype(jnp.bfloat16)
-    image = lax.all_gather(image_part, "mp", axis=1, tiled=True)
+    shares = lax.axis_size("mp")
+    gallery = [(idx, (idx + 1) % shares) for idx in range(shares)]
+    windows = [image_part]
+    while len(windows) < shares:
+        windows.append(lax.ppermute(windows[-1], perm=gallery, axis_name="mp"))
+    b_next = lax.axis_index("mp")
+    windows = jnp.stack(windows, axis=0)[(b_next - jnp.arange(shares)) % shares]
+    image = state_manage(windows, 1)
     width_k = key_full.shape[1]
     keys_raw = jnp.dot(image, key_full, preferred_element_type=jnp.float32).reshape(
         slot_rows, width_k // HD, HD

time: 706 us -> 656 us (0.929)
  waiting for transfers between devices: 561 us -> 487 us
  local copies, waits for them, and re-layouts: 51.3 us -> 64.2 us
    ppermute x0 -> x3, waiting for transfers between devices: none -> 79.1 us  [per_device(): windows.append(lax.ppermute(windows[-1], perm=gallery, axis_name='mp'))]
    all_gather x1 -> x0, waiting for transfers between devices: 76.4 us -> none  [per_device(): image = lax.all_gather(image_part, 'mp', axis=1, tiled=True)]
    all_gather x1, waiting for transfers between devices: 140 us -> 84 us  [per_device(): full_text = lax.all_gather(arrived, 'mp', axis=3, tiled=True)[0, 0]]
    all_gather x1, waiting for transfers between devices: 34.7 us -> 0.02 us  [per_device(): shard_piece = lax.all_gather(vision, 'section', axis=1, tiled=True)]
    ppermute x1, waiting for transfers between devices: 47.3 us -> 68.3 us  [shifted(): return lax.ppermute(value, axis, pairs)]
  transfers between devices with their start and end apart: 10 -> 12, of which waited for: 9 -> 9; matrix products, arithmetic and copies ran while one was open for 10% -> 13% of each run, Pallas kernels for 0% -> 0%
where the time goes in v1:
time: 656 us; the launch traced here: 654 us
  waiting for transfers between devices  487 us (74%)
  local copies, waits for them, and re-layouts  64.2 us (10%)
  matrix products  47.6 us (7%)
  other arithmetic  33 us (5%)
  between operations  17.8 us (3%)
    all_gather x1, waiting for transfers between devices, per_device(): lax.all_gather(query_weight, 'dp', axis=1, tiled=True)[0]  100 us
    all_gather x1, waiting for transfers between devices, per_device(): full_text = lax.all_gather(arrived, 'mp', axis=3, tiled=True)[0, 0]  84 us
    ppermute x3, waiting for transfers between devices, per_device(): windows.append(lax.ppermute(windows[-1], perm=gallery, axis_name='mp'))  79.1 us
    ppermute x1, waiting for transfers between devices, shifted(): return lax.ppermute(value, axis, pairs)  68.3 us
    reduce_scatter x1, waiting for transfers between devices, per_device(): lax.psum_scatter(jnp.concatenate([key_part, value_part], axis=1).astype(j...  62.2 us
    reduce_scatter x1, waiting for transfers between devices, per_device(): lax.psum_scatter(partial_bf.astype(jnp.float32).astype(jnp.bfloat16), 'mp...  59.6 us
    reduce_scatter x1, waiting for transfers between devices, per_device(): lax.psum_scatter(jnp.where((row_ids // slot_rows == wanted)[:, None], tak...  30.4 us
    dot_general x1, local copies, waits for them, and re-layouts, per_device(): jnp.dot(columns, lax.all_gather(query_weight, 'dp', axis=1, tiled=True)[0...  21.4 us
  transfers between devices with their start and end apart: 12, of which 9 were waited for; matrix products, arithmetic and copies ran while one was open for 13% of the time, Pallas kernels for 0%

profile of v1, /device:TPU:0, one launch (start us, length us, event | category | flops | bytes accessed | tf_op | source)
XLA Modules:
  0.0 654.3 jit_solution(1845855658397188529)
XLA Ops:
  8.0 0.7 all-gather.10.cloned.1.call-update
  9.4 3.0 collective-permute-start.3
  12.4 68.3 %collective-permute-done.3 = bf16[1,1,512,2048]{3,2,1,0:T(8,128)(2,1)S(1)} collective-permute-done((bf16[1,1,512,2048]{3,2,1,0:T(8,128)(2,1)}, bf16[1,1,512,2048]{3,2,1,0:T(8,128)(2,1)S(1)}, u32[]{:S(2)}, u32[]{:S(2)}) %collective-permute-start.3) | collective-permute-done | bytes 2097184 | tf_op jit(solution)/shard_map/ppermute | solution.py:19
  80.8 1.4 copy-done.9
  84.1 2.5 fusion.30
  86.6 1.9 collective-permute-start
  88.4 24.3 %collective-permute-done = bf16[256,2048]{1,0:T(8,128)(2,1)S(1)} collective-permute-done((bf16[256,2048]{1,0:T(8,128)(2,1)S(1)}, bf16[256,2048]{1,0:T(8,128)(2,1)S(1)}, u32[]{:S(2)}, u32[]{:S(2)}) %collective-permute-start) | collective-permute-done | bytes 1048608 | tf_op jit(solution)/shard_map/ppermute | solution.py:94
  112.8 1.0 copy-done.10
  113.7 25.3 %collective-permute-done.1 = bf16[256,2048]{1,0:T(8,128)(2,1)} collective-permute-done((bf16[256,2048]{1,0:T(8,128)(2,1)S(1)}, bf16[256,2048]{1,0:T(8,128)(2,1)}, u32[]{:S(2)}, u32[]{:S(2)}) %collective-permute-start.1) | collective-permute-done | bytes 1048608 | tf_op jit(solution)/shard_map/ppermute | solution.py:94
  140.3 1.5 copy.107
  144.4 1.2 iota_compare_fusion.1
  145.6 29.5 %collective-permute-done.2 = bf16[256,2048]{1,0:T(8,128)(2,1)} collective-permute-done((bf16[256,2048]{1,0:T(8,128)(2,1)}, bf16[256,2048]{1,0:T(8,128)(2,1)}, u32[]{:S(2)}, u32[]{:S(2)}) %collective-permute-start.2) | collective-permute-done | bytes 1048608 | tf_op jit(solution)/shard_map/ppermute | solution.py:94
  175.1 3.6 pad_maximum_fusion.1
  178.7 5.0 gather_fusion
  183.7 6.3 copy.69
  189.9 6.4 copy.72
  196.3 4.8 multiply_reduce_fusion.2
  201.1 0.7 multiply_convert_fusion.1
  201.9 6.4 copy.70
  208.3 4.8 convolution_convert_fusion.2
  213.1 2.1 fusion.39
  215.1 84.0 %all-gather.12.cloned.1.call-done = bf16[1,1,512,8192]{3,2,1,0:T(8,128)(2,1)} async-done(((bf16[1,1,512,2048]{3,2,1,0:T(8,128)(2,1)}), bf16[1,1,512,8192]{3,2,1,0:T(8,128)(2,1)}) %all-gather.12.cloned.1.call-update) | async-done | bytes 8388624 | tf_op jit(solution)/shard_map/all_gather | solution.py:63
  299.2 5.1 fusion.1
  304.3 100.4 %all-gather.14.cloned.1.call-done = bf16[1,8192,1024]{2,1,0:T(8,128)(2,1)} async-done(((bf16[1,2048,1024]{2,1,0:T(8,128)(2,1)}), bf16[1,8192,1024]{2,1,0:T(8,128)(2,1)}) %all-gather.14.cloned.1.call-update) | async-done | bytes 16777232 | tf_op jit(solution)/shard_map/all_gather | solution.py:70
  404.6 21.4 %copy.74 = bf16[1024,8192]{1,0:T(8,128)(2,1)} copy(bf16[1024,8192]{0,1:T(8,128)(2,1)} %bitcast.158) | data formatting | bytes 33554432 | tf_op jit(solution)/shard_map/dot_general | solution.py:68
  426.1 14.8 %multiply_reduce_fusion = (f32[512,8]{0,1:T(8,128)S(1)}, f32[512,8,128]{0,2,1:T(8,128)S(1)}) fusion(bf16[8,128,8192]{2,1,0:T(8,128)(2,1)} %bitcast.159, bf16[1,1,512,8192]{3,2,1,0:T(8,128)(2,1)} %all-gather.12.cloned.1.call-done, f32[8192]{0:T(1024)S(1)} %bitcast.180, f32[512]{0:T(512)S(1)} %add_rsqrt_fusion.1), kind=kOutput, calls=%fused_computation.53 | convolution fusion | flops 8607756288 | bytes 27314176 | tf_op jit(solution)/shard_map/dot_general | solution.py:68
  441.4 5.1 fusion.96
  446.5 0.7 multiply_divide_fusion
  447.2 3.9 fusion.16
  451.1 0.7 copy-done.8
  451.9 1.2 fusion.59
  453.4 0.9 fusion.56
  454.2 1.0 copy-done.5
  455.3 1.3 fusion.19
  456.6 0.9 copy-done.6
  457.5 3.4 fusion.4
  460.9 5.6 convolution_convert_fusion
  466.5 3.2 convolution_convert_fusion.1
  469.8 7.7 %pad_maximum_fusion = bf16[8192,512]{0,1:T(8,128)(2,1)} fusion(bf16[8192,256]{0,1:T(8,128)(2,1)} %convolution_convert_fusion, bf16[8192,256]{0,1:T(8,128)(2,1)} %convolution_convert_fusion.1), kind=kLoop, calls=%fused_computation.14 | loop fusion | flops 16777216 | bytes 16777216 | tf_op jit(solution)/shard_map/concatenate | solution.py:143
  478.2 59.6 %reduce-scatter.4.cloned.1.call-done = bf16[256,2048]{1,0:T(8,128)(2,1)} async-done(((bf16[256,8192]{1,0:T(8,128)(2,1)}), bf16[256,2048]{1,0:T(8,128)(2,1)}) %reduce-scatter.4.cloned.1.call-update) | async-done | bytes 1048592 | tf_op jit(solution)/shard_map/reduce_scatter | solution.py:122
  537.8 6.8 %gather_fusion.1 = bf16[512,2048]{1,0:T(8,128)(2,1)} fusion(bf16[256,2048]{1,0:T(8,128)(2,1)} %reduce-scatter.4.cloned.1.call-done, s32[1024]{0:T(1024)S(1)} %pad_clamp_fusion), kind=kCustom, calls=%fused_computation.1 | custom fusion | bytes 4196352 | tf_op jit(solution)/shard_map/jit(_take)/gather | solution.py:126
  544.6 3.7 select_convert_fusion
  549.4 1.2 select_convert_fusion.1
  550.6 62.2 %reduce-scatter.8.cloned.1.call-done = bf16[2048,512]{0,1:T(8,128)(2,1)} async-done(((bf16[8192,512]{0,1:T(8,128)(2,1)}), bf16[2048,512]{0,1:T(8,128)(2,1)}) %reduce-scatter.8.cloned.1.call-update) | async-done | bytes 2097168 | tf_op jit(solution)/shard_map/reduce_scatter | solution.py:142
  612.8 1.7 slice_bitcast_fusion
  614.5 1.3 copy.86
  615.8 1.3 copy.87
  617.1 30.4 %reduce-scatter.6.cloned.1.call-done = bf16[256,2048]{1,0:T(8,128)(2,1)} async-done(((bf16[512,2048]{1,0:T(8,128)(2,1)}), bf16[256,2048]{1,0:T(8,128)(2,1)}) %reduce-scatter.6.cloned.1.call-update) | async-done | bytes 1048592 | tf_op jit(solution)/shard_map/reduce_scatter | solution.py:127
  (69 shorter events, 6.7 us)
Async XLA Ops:
  7.2 75.7 %copy-start = (s32[1,2]{1,0:T(1,128)S(1)}, s32[1,2]{1,0:T(1,128)}, u32[]{:S(2)}) copy-start(s32[1,2]{1,0:T(1,128)} %param.17) | copy-start | bytes 28
  7.2 76.9 %all-gather.6.cloned.1.call-start = ((), (), s32[]{:S(2)}) async-start(), calls=%async_computation.3 | async-start | bytes 3145728 | tf_op jit(solution)/shard_map/all_gather | solution.py:85
  7.9 182.0 %all-gather.10.cloned.1.call-start = ((), (), s32[]{:S(2)}) async-start(), calls=%async_computation.5 | async-start | bytes 5242880 | tf_op jit(solution)/shard_map/all_gather | solution.py:77
  8.7 193.2 %all-gather.8.cloned.1.call-start = ((), (), s32[]{:S(2)}) async-start(), calls=%async_computation.4 | async-start | bytes 5242880 | tf_op jit(solution)/shard_map/all_gather | solution.py:78
  9.4 289.8 %all-gather.12.cloned.1.call-start = ((), (), s32[]{:S(2)}) async-start(), calls=%async_computation.6 | async-start | bytes 10485760 | tf_op jit(solution)/shard_map/all_gather | solution.py:63
  9.4 71.3 %collective-permute-start.3 = (bf16[1,1,512,2048]{3,2,1,0:T(8,128)(2,1)}, bf16[1,1,512,2048]{3,2,1,0:T(8,128)(2,1)S(1)}, u32[]{:S(2)}, u32[]{:S(2)}) collective-permute-start(bf16[1,1,512,2048]{3,2,1,0:T(8,128)(2,1)} %param.13), channel_id=1, source_target_pairs={{0,16},{16,0},{1,17},{17,1},{2,18},{18,2},{3,19},{19,3},{4,20},{20... | collective-permute-start | bytes 6291464 | tf_op jit(solution)/shard_map/ppermute | solution.py:19
  80.8 1.4 copy-start.9
  82.2 322.5 %all-gather.14.cloned.1.call-start = ((), (), s32[]{:S(2)}) async-start(), calls=%async_computation.7 | async-start | bytes 20971520 | tf_op jit(solution)/shard_map/all_gather | solution.py:70
  82.8 61.1 %copy-start.15 = (s32[1,2]{1,0:T(1,128)S(1)}, s32[1,2]{1,0:T(1,128)}, u32[]{:S(2)}) copy-start(s32[1,2]{1,0:T(1,128)} %param.15) | copy-start | bytes 28
  82.8 455.0 %reduce-scatter.4.cloned.1.call-start = ((), (), s32[]{:S(2)}) async-start(), calls=%async_computation.8 | async-start | bytes 5242880 | tf_op jit(solution)/shard_map/reduce_scatter | solution.py:122
  86.6 26.2 %collective-permute-start = (bf16[256,2048]{1,0:T(8,128)(2,1)S(1)}, bf16[256,2048]{1,0:T(8,128)(2,1)S(1)}, u32[]{:S(2)}, u32[]{:S(2)}) collective-permute-start(bf16[256,2048]{1,0:T(8,128)(2,1)S(1)} %fusion.30), channel_id=1, source_target_pairs={{0,4},{4,8},{8,12},{12,0},{1,5},{5,9},{9,13},{13,1},{2,6},{6,10},{... | collective-permute-start | bytes 3145736 | tf_op jit(solution)/shard_map/ppermute | solution.py:94
  112.8 1.0 copy-start.10
  113.7 25.3 %collective-permute-start.1 = (bf16[256,2048]{1,0:T(8,128)(2,1)S(1)}, bf16[256,2048]{1,0:T(8,128)(2,1)}, u32[]{:S(2)}, u32[]{:S(2)}) collective-permute-start(bf16[256,2048]{1,0:T(8,128)(2,1)S(1)} %collective-permute-done), channel_id=1, source_target_pairs={{0,4},{4,8},{8,12},{12,0},{1,5},{5,9},{9,13},{13,1},{2,6},{6,10},{... | collective-permute-start | bytes 3145736 | tf_op jit(solution)/shard_map/ppermute | solution.py:94
  139.0 36.1 %collective-permute-start.2 = (bf16[256,2048]{1,0:T(8,128)(2,1)}, bf16[256,2048]{1,0:T(8,128)(2,1)}, u32[]{:S(2)}, u32[]{:S(2)}) collective-permute-start(bf16[256,2048]{1,0:T(8,128)(2,1)} %collective-permute-done.1), channel_id=1, source_target_pairs={{0,4},{4,8},{8,12},{12,0},{1,5},{5,9},{9,13},{13,1},{2,6},{6,10},{... | collective-permute-start | bytes 3145736 | tf_op jit(solution)/shard_map/ppermute | solution.py:94
  196.3 4.8 copy-start.12
  404.6 21.4 %copy-start.14 = (f32[1,8192]{1,0:T(1,128)S(1)}, f32[1,8192]{1,0:T(1,128)}, u32[]{:S(2)}) copy-start(f32[1,8192]{1,0:T(1,128)} %param.18) | copy-start | bytes 98308
  426.1 14.8 %copy-start.13 = (f32[1,128]{1,0:T(1,128)S(1)}, f32[1,128]{1,0:T(1,128)}, u32[]{:S(2)}) copy-start(f32[1,128]{1,0:T(1,128)} %param.22) | copy-start | bytes 1540
  447.2 3.9 copy-start.7
  447.2 4.7 copy-start.8
  447.2 4.7 copy-start.11
  447.2 4.7 copy-start.16
  451.1 2.3 copy-start.3
  453.1 2.2 copy-start.5
  455.3 2.2 copy-start.6
  460.9 151.9 %reduce-scatter.8.cloned.1.call-start = ((), (), s32[]{:S(2)}) async-start(), calls=%async_computation.10 | async-start | bytes 10485760 | tf_op jit(solution)/shard_map/reduce_scatter | solution.py:142
  460.9 5.6 copy-start.2
  477.5 170.0 %reduce-scatter.6.cloned.1.call-start = ((), (), s32[]{:S(2)}) async-start(), calls=%async_computation.9 | async-start | bytes 3145728 | tf_op jit(solution)/shard_map/reduce_scatter | solution.py:127
  544.6 3.7 copy-start.4
  549.4 98.1 %copy-start.1 = (s32[1,2]{1,0:T(1,128)S(1)}, s32[1,2]{1,0:T(1,128)}, u32[]{:S(2)}) copy-start(s32[1,2]{1,0:T(1,128)} %param.17) | copy-start | bytes 28
Sparse Core Ops, SparseCore 0:
  9.6 58.3 all-gather.5
  69.6 34.4 all-gather.9
  105.6 34.4 all-gather.7
  141.6 157.5 all-gather.11
  300.6 104.0 all-gather.13
  461.0 76.7 reduce-scatter.3
  540.6 72.2 reduce-scatter.7
  615.6 31.8 reduce-scatter.5
